TPU v7x, 256 devices: a whole 4x4x8 slice. The times are simulated.
256 devices in a mesh: row: 32 (over z, x), col: 8 (over y, core).
Axes of the slice: x: 4, y: 4, z: 8, core: 2. Of those that a mesh axis runs over, the one named last changes fastest.
Arguments:
- x_points: bfloat16 [32768, 64], P(('row', 'col')), may hold values from -6 to 6
- y_points: bfloat16 [65536, 64], P(('col', 'row')), may hold values from -6 to 6
- row_mass: bfloat16 [32768], P(('row', 'col')), may hold values from 1 to 30, as said below
- col_mass: bfloat16 [65536], P(('col', 'row')), may hold values from 1 to 30, as said below
- multipliers: bfloat16 [32768, 64], P(('row', 'col')), may hold values from -12 to 12
- col_potential: bfloat16 [65536], P(('col', 'row')), may hold values from -3 to 3
- basket: float32 [64], replicated, may hold values from 0.05 to 0.25
- damping: float32 [64], replicated, may hold values from 0.3 to 1.5
Outputs:
- row_potential: float32 [32768], P('row')
- col_potential_new: float32 [65536], P('col')
- multipliers_new: float32 [32768, 64], P(('row', 'col'))
Inputs may be any that keep to these rules, and one draw needn't show every extreme that they name: `row_mass`: weights rise along the points' order by up to a factor of three. `col_mass`: weights rise along the points' order by up to a factor of three.
All inputs are finite; a program needn't handle non-finite values.
Results may differ from a plain program's by a relative error of at most 0.0012.
Values may be sent and summed in bfloat16 or wider, within the bound.
No kernel may reach another device: no remote copies, remote signals or barrier semaphores. Data moves between devices by JAX's collectives and lax.ppermute only.
A program may use at most 64 MiB of HBM per device.

v0:
```python
import jax
import jax.numpy as jnp
from jax import lax
from jax.sharding import PartitionSpec as P

EPS = 0.5
KAPPA = 0.5
RIDGE = 1.0


def joined(value, axis, join):
    pieces = jax.tree.map(lambda part: lax.all_gather(part, axis), value)
    head = jax.tree.map(lambda part: part[0], pieces)
    tail = jax.tree.map(lambda part: part[1:], pieces)
    subtotal, _ = lax.scan(lambda subtotal, piece: (join(subtotal, piece), None), head, tail)
    return subtotal


def prepare_rows(x_rows, mult_rows, basket):
    xf = x_rows.astype(jnp.float32)
    hf = mult_rows.astype(jnp.float32)
    width = xf.shape[1]
    query = hf + 2.0 * KAPPA / width * xf
    row_term = -jnp.sum(hf * xf, axis=1) - KAPPA / width * jnp.sum(xf * xf, axis=1)
    row_basket = jnp.sum(xf * basket[None, :], axis=1)
    return (query, row_term, row_basket)


def prepare_cols(y_cols, basket):
    yf = y_cols.astype(jnp.float32)
    width = yf.shape[1]
    col_term = -(KAPPA / width) * jnp.sum(yf * yf, axis=1)
    col_basket = jnp.sum(yf * basket[None, :], axis=1)
    features = jnp.concatenate([yf, yf * yf], axis=1).astype(jnp.bfloat16)
    return (yf, col_term, col_basket, features)


def scores(query, row_term, row_basket, y_float, col_term, col_basket):
    dots = lax.dot_general(
        query,
        y_float,
        (((1,), (1,)), ((), ())),
        precision=lax.Precision.HIGHEST,
        preferred_element_type=jnp.float32,
    )
    payoff = jax.nn.relu(col_basket[None, :] - row_basket[:, None])
    return (dots + row_term[:, None] + col_term[None, :] + payoff) / EPS


def lse_join(first, second):
    top = jnp.maximum(first[0], second[0])
    total = first[1] * jnp.exp(first[0] - top) + second[1] * jnp.exp(second[0] - top)
    return (top, total)


def on_device(x_points, y_points, row_mass, col_mass, multipliers, col_potential, basket, damping):
    x_rows, mult_rows, mass_rows = (
        lax.all_gather(x_points, "col", axis=0, tiled=True),
        lax.all_gather(multipliers, "col", axis=0, tiled=True),
        lax.all_gather(row_mass, "col", axis=0, tiled=True),
    )
    y_cols, pot_cols, mass_cols = (
        lax.all_gather(y_points, "row", axis=0, tiled=True),
        lax.all_gather(col_potential, "row", axis=0, tiled=True),
        lax.all_gather(col_mass, "row", axis=0, tiled=True),
    )
    query, row_term, row_basket = prepare_rows(x_rows, mult_rows, basket)
    y_float, col_term, col_basket, features = prepare_cols(y_cols, basket)
    row_weight = mass_rows.astype(jnp.float32)
    col_weight = mass_cols.astype(jnp.float32)
    log_row = jnp.log(row_weight)
    log_col = jnp.log(col_weight)
    nrows = x_rows.shape[0]
    block = min(128, nrows)
    count = nrows // block
    starts = jnp.arange(count, dtype=jnp.int32) * block

    def cut(arr, start):
        return lax.dynamic_slice_in_dim(arr, start, block, 0)

    def block_scores(start):
        return scores(
            cut(query, start),
            cut(row_term, start),
            cut(row_basket, start),
            y_float,
            col_term,
            col_basket,
        )

    gshift = pot_cols.astype(jnp.float32) / EPS + log_col

    def row_pass(start):
        z = block_scores(start) + gshift[None, :]
        top = jnp.max(z, axis=1)
        total = jnp.sum(jnp.exp(z - top[:, None]), axis=1)
        return (top, total)

    row_tops, row_totals = lax.map(row_pass, starts)
    row_tops = row_tops.reshape(nrows)
    row_totals = row_totals.reshape(nrows)
    mu_total, nu_total = lax.psum(
        (jnp.sum(row_mass.astype(jnp.float32)), jnp.sum(col_mass.astype(jnp.float32))),
        ("row", "col"),
    )
    row_top, row_total = joined((row_tops, row_totals), "col", lse_join)
    log_nu_total = jnp.log(nu_total)
    row_potential = -EPS * (row_top + jnp.log(row_total) - log_nu_total)
    fshift = row_potential / EPS + log_row

    def col_pass(start):
        z = block_scores(start) + cut(fshift, start)[:, None]
        top = jnp.max(z, axis=0)
        total = jnp.sum(jnp.exp(z - top[None, :]), axis=0)
        return (top, total)

    col_tops, col_totals = lax.map(col_pass, starts)
    col_top = jnp.max(col_tops, axis=0)
    col_total = jnp.sum(col_totals * jnp.exp(col_tops - col_top[None, :]), axis=0)
    peak = lax.pmax(col_top, "row")
    scaled = col_total * jnp.exp(col_top - peak)
    whole = lax.psum(scaled, "row")
    col_potential_new = -EPS * (peak + jnp.log(whole) - jnp.log(mu_total))
    gq = col_potential_new / EPS + log_col - log_nu_total
    fq = row_potential / EPS

    def moment_pass(start):
        plan = jnp.exp(block_scores(start) + cut(fq, start)[:, None] + gq[None, :]).astype(
            jnp.bfloat16
        )
        both = jnp.dot(plan, features, preferred_element_type=jnp.float32)
        mass = jnp.sum(plan.astype(jnp.float32), axis=1)
        return (both, mass)

    both, mass = lax.map(moment_pass, starts)
    both = both.reshape(nrows, features.shape[1])
    mass = mass.reshape(nrows)
    share = x_points.shape[0]
    both_all, mass_all = lax.psum((both, mass), "col")
    offset = lax.axis_index("col") * share
    own_both = lax.dynamic_slice_in_dim(both_all, offset, share, 0)
    own_mass = lax.dynamic_slice_in_dim(mass_all, offset, share, 0)
    width = x_points.shape[1]
    first = own_both[:, :width]
    second = own_both[:, width:]
    xf = x_points.astype(jnp.float32)
    grad = first - xf * own_mass[:, None]
    curv = (second - 2.0 * xf * first + xf * xf * own_mass[:, None]) / EPS + RIDGE
    multipliers_new = multipliers.astype(jnp.float32) - damping[None, :] * grad / curv
    return (row_potential, col_potential_new, multipliers_new)


def solution(mesh):
    placed = (
        P(("row", "col"), None),
        P(("col", "row"), None),
        P(("row", "col")),
        P(("col", "row")),
        P(("row", "col"), None),
        P(("col", "row")),
        P(),
        P(),
    )
    return jax.shard_map(
        on_device,
        mesh=mesh,
        in_specs=placed,
        out_specs=(P("row"), P("col"), P(("row", "col"), None)),
        check_vma=False,
    )
```

profile of v0, /device:TPU:2, one launch (start us, length us, event | category | flops | bytes accessed | tf_op | source)
XLA Modules:
  0.0 851.1 jit_solution(13461661143674850518)
XLA Ops:
  7.2 1.5 copy.17
  8.8 1.3 convert_reduce_fusion.1
  10.0 1.3 convert_reduce_fusion.2
  11.3 79.4 %all-reduce = (f32[]{:T(128)}, f32[]{:T(128)}) all-reduce(f32[]{:T(128)} %convert_reduce_fusion.1, f32[]{:T(128)} %convert_reduce_fusion.2), channel_id=1, replica_groups=mesh['row'=32,'col'=8] {'row','col'}, use_global_device_ids=true, to_apply=%region_12.13 | all-reduce | flops 2 | bytes 16 | tf_op jit(solution)/shard_map/psum | solution.py:102
  95.0 42.6 %all-gather.1 = bf16[32,1,256]{2,1,0:T(2,128)(2,1)S(1)} all-gather(bf16[1,1,256]{2,1,0:T(2,128)(2,1)S(1)} %reshape.38), channel_id=1, replica_groups=mesh['row'=32,'col'=8] {'row'}, dimensions={0}, use_global_device_ids=true | all-gather | bytes 16896 | tf_op jit(solution)/shard_map/all_gather | solution.py:65
  137.6 40.5 %all-gather = bf16[32,1,256]{2,1,0:T(2,128)(2,1)S(1)} all-gather(bf16[1,1,256]{2,1,0:T(2,128)(2,1)S(1)} %reshape.36), channel_id=1, replica_groups=mesh['row'=32,'col'=8] {'row'}, dimensions={0}, use_global_device_ids=true | all-gather | bytes 16896 | tf_op jit(solution)/shard_map/all_gather | solution.py:64
  178.2 9.2 %all-gather.4 = bf16[8,1,128]{2,1,0:T(2,128)(2,1)S(1)} all-gather(bf16[1,1,128]{2,1,0:T(2,128)(2,1)} %bitcast.86), channel_id=1, replica_groups=mesh['row'=32,'col'=8] {'col'}, dimensions={0}, use_global_device_ids=true | all-gather | bytes 2304 | tf_op jit(solution)/shard_map/all_gather | solution.py:60
  187.4 12.8 %all_gather.24 = bf16[1024,64]{1,0:T(8,128)(2,1)S(1)} all-gather(bf16[128,64]{1,0:T(8,128)(2,1)S(1)} %copy.15), channel_id=1, replica_groups=mesh['row'=32,'col'=8] {'col'}, dimensions={0}, use_global_device_ids=true | all-gather | bytes 147456 | tf_op jit(solution)/shard_map/all_gather | solution.py:59
  200.2 12.8 %all_gather.25 = bf16[1024,64]{1,0:T(8,128)(2,1)S(1)} all-gather(bf16[128,64]{1,0:T(8,128)(2,1)S(1)} %copy.16), channel_id=1, replica_groups=mesh['row'=32,'col'=8] {'col'}, dimensions={0}, use_global_device_ids=true | all-gather | bytes 147456 | tf_op jit(solution)/shard_map/all_gather | solution.py:58
  213.1 1.2 fusion.24
  214.3 5.2 multiply_reduce_fusion
  219.5 2.2 convert_element_type.39
  221.7 80.0 %while.48 = (s32[]{:T(128)}, f32[8,128]{1,0:T(8,128)S(1)}, f32[8,128]{1,0:T(8,128)S(1)}, s32[8]{0:T(128)S(1)}, f32[1024,64]{1,0:T(8,128)S(1)}, /*index=5*/f32[81...) while((s32[]{:T(128)}, f32[8,128]{1,0:T(8,128)S(1)}, ...), condition=%wide.region_8.9_spmd, body=%wide.region_5.8_spmd.sunk | while | flops 815791872 | bytes 10656463 | solution.py:99
  224.4 6.5 fusion.52
  234.4 6.5 fusion.52
  244.4 6.5 fusion.52
  254.4 6.5 fusion.52
  264.4 6.5 fusion.52
  274.4 6.5 fusion.52
  284.4 6.5 fusion.52
  294.4 6.5 fusion.52
  301.7 12.9 %all-gather.2 = f32[8,1,1024]{2,1,0:T(1,128)S(1)} all-gather(f32[1,1,1024]{2,1,0:T(1,128)S(1)} %bitcast.83), channel_id=1, replica_groups=mesh['row'=32,'col'=8] {'col'}, dimensions={0}, use_global_device_ids=true | all-gather | bytes 36864 | tf_op jit(solution)/shard_map/all_gather | solution.py:12
  314.7 13.1 %all-gather.3 = f32[8,1,1024]{2,1,0:T(1,128)S(1)} all-gather(f32[1,1,1024]{2,1,0:T(1,128)S(1)} %bitcast.82), channel_id=1, replica_groups=mesh['row'=32,'col'=8] {'col'}, dimensions={0}, use_global_device_ids=true | all-gather | bytes 36864 | tf_op jit(solution)/shard_map/all_gather | solution.py:12
  328.7 80.8 %while.50 = (s32[]{:T(128)}, f32[8,8192]{1,0:T(8,128)S(1)}, f32[8,8192]{1,0:T(8,128)S(1)}, s32[8]{0:T(128)S(1)}, f32[1024,64]{1,0:T(8,128)S(1)}, /*index=5*/f32[...) while((s32[]{:T(128)}, f32[8,8192]{1,0:T(8,128)S(1)}, ...), condition=%wide.region_16.17_spmd, body=%wide.region_13.16_spmd.sunk | while | flops 815775744 | bytes 10851027 | solution.py:117
  331.5 6.4 fusion.54
  341.6 6.4 fusion.54
  351.7 6.4 fusion.54
  361.8 6.4 fusion.54
  371.9 6.4 fusion.54
  382.0 6.4 fusion.54
  392.1 6.4 fusion.54
  402.2 6.4 fusion.54
  409.7 136.0 %pmax.7 = f32[8192]{0:T(1024)S(1)} all-reduce(f32[8192]{0:T(1024)S(1)} %reduce_max.27), channel_id=1, replica_groups=mesh['row'=32,'col'=8] {'row'}, use_global_device_ids=true, to_apply=%region_18.19 | all-reduce | flops 8192 | bytes 65536 | tf_op jit(solution)/shard_map/pmax | solution.py:120
  545.8 139.9 %psum.36 = f32[8192]{0:T(1024)S(1)} all-reduce(f32[8192]{0:T(1024)S(1)} %exponential_multiply_fusion), channel_id=1, replica_groups=mesh['row'=32,'col'=8] {'row'}, use_global_device_ids=true, to_apply=%region_20.21 | all-reduce | flops 8192 | bytes 65536 | tf_op jit(solution)/shard_map/psum | solution.py:122
  686.4 3.4 pad_maximum_fusion
  689.8 88.4 %while.51 = (s32[]{:T(128)}, f32[8,128,128]{2,1,0:T(8,128)S(1)}, f32[8,128]{1,0:T(8,128)S(1)}, s32[8]{0:T(128)S(1)}, f32[1024,64]{1,0:T(8,128)S(1)}, /*index=5*/...) while((s32[]{:T(128)}, f32[8,128,128]{2,1,0:T(8,128)S(1)}, ...), condition=%wide.region_25.26_spmd, body=%wide.region_23.25_spmd.sunk | while | flops 1085276032 | bytes 8624355 | solution.py:135
  692.5 7.5 convert_reduce_fusion.4
  703.6 7.5 convert_reduce_fusion.4
  714.6 7.5 convert_reduce_fusion.4
  725.7 7.5 convert_reduce_fusion.4
  736.7 7.5 convert_reduce_fusion.4
  747.8 7.5 convert_reduce_fusion.4
  758.8 7.5 convert_reduce_fusion.4
  769.9 7.5 convert_reduce_fusion.4
  778.1 1.0 copy.19
  779.2 12.4 %psum.39 = f32[1024]{0:T(1024)S(1)} all-reduce(f32[1024]{0:T(1024)S(1)} %bitcast.84), channel_id=1, replica_groups=mesh['row'=32,'col'=8] {'col'}, use_global_device_ids=true, to_apply=%region_27.28 | all-reduce | flops 1024 | bytes 8192 | tf_op jit(solution)/shard_map/psum | solution.py:139
  791.7 51.1 %all-reduce.3.cloned.1.call-done = f32[1024,128]{0,1:T(8,128)} async-done(((f32[1024,128]{0,1:T(8,128)}), f32[1024,128]{0,1:T(8,128)}) %all-reduce.3.cloned.1.call-update) | async-done | bytes 524304 | tf_op jit(solution)/shard_map/psum | solution.py:139
  842.8 1.5 fusion.28
  (209 shorter events, 44.4 us)
Async XLA Ops:
  7.2 207.1 %all-gather.7.cloned.1.call-start = ((), (), s32[]{:S(2)}) async-start(), calls=%async_computation | async-start | bytes 2162688 | tf_op jit(solution)/shard_map/all_gather | solution.py:63
  8.7 834.1 %all-reduce.3.cloned.1.call-start = ((), (), s32[]{:S(2)}) async-start(), calls=%async_computation.1 | async-start | bytes 1048576 | tf_op jit(solution)/shard_map/psum | solution.py:139
  214.3 5.2 copy-start
  689.7 153.1 %copy-start.1 = (bf16[128,64]{0,1:T(8,128)(2,1)S(1)}, bf16[128,64]{0,1:T(8,128)(2,1)}, u32[]{:S(2)}) copy-start(bf16[128,64]{0,1:T(8,128)(2,1)} %param.16) | copy-start | bytes 49156
  689.7 153.1 %copy-start.2 = (bf16[128,64]{0,1:T(8,128)(2,1)S(1)}, bf16[128,64]{0,1:T(8,128)(2,1)}, u32[]{:S(2)}) copy-start(bf16[128,64]{0,1:T(8,128)(2,1)} %param.20) | copy-start | bytes 49156
  689.8 153.1 %copy-start.3 = (f32[64]{0:T(128)S(1)}, f32[64]{0:T(128)}, u32[]{:S(2)}) copy-start(f32[64]{0:T(128)} %param.23) | copy-start | bytes 772
Sparse Core Ops, SparseCore 0:
  10.6 79.5 all-gather.6
  779.3 63.4 all-reduce.2
where the time goes:
time: 853 us; the launch traced here: 851 us
  blocking collectives  512 us (60%)
  matrix products  169 us (20%)
  waiting for transfers between devices  51.2 us (6%)
  loops' own time  47.5 us (6%)
  other arithmetic  28.6 us (3%)
  local copies, waits for them, and re-layouts  27.8 us (3%)
  between operations  15.6 us (2%)
    dot_general x24, matrix products, scores(): lax.dot_general(query, y_float, (((1,), (1,)), ((), ())), precision=lax.P...  163 us
    psum x1, blocking collectives, on_device(): whole = lax.psum(scaled, 'row')  140 us
    pmax x1, blocking collectives, on_device(): peak = lax.pmax(col_top, 'row')  136 us
    psum x1, blocking collectives, on_device(): lax.psum((jnp.sum(row_mass.astype(jnp.float32)), jnp.sum(col_mass.astype(...  79.4 us
    psum x1, waiting for transfers between devices, on_device(): both_all, mass_all = lax.psum((both, mass), 'col')  51.1 us
    all_gather x1, blocking collectives, on_device(): lax.all_gather(col_mass, 'row', axis=0, tiled=True)  42.6 us
    all_gather x1, blocking collectives, on_device(): lax.all_gather(col_potential, 'row', axis=0, tiled=True)  40.5 us
    all_gather x2, blocking collectives, joined(): pieces = jax.tree.map(lambda part: lax.all_gather(part, axis), value)  26 us
  transfers between devices with their start and end apart: 2, of which 1 were waited for; matrix products, arithmetic and copies ran while one was open for 1% of the time, Pallas kernels for 0%

commit v1 on v0

--- a/solution.py
+++ b/solution.py
@@ -6,6 +6,10 @@
 EPS = 0.5
 KAPPA = 0.5
 RIDGE = 1.0
+
+
+def step_on_ratios(block_here, peer_axis):
+    return jnp.sum(lax.all_gather(block_here, axis_name=peer_axis), axis=0)
 
 
 def joined(value, axis, join):
@@ -119,7 +123,7 @@
     col_total = jnp.sum(col_totals * jnp.exp(col_tops - col_top[None, :]), axis=0)
     peak = lax.pmax(col_top, "row")
     scaled = col_total * jnp.exp(col_top - peak)
-    whole = lax.psum(scaled, "row")
+    whole = step_on_ratios(scaled, "row")
     col_potential_new = -EPS * (peak + jnp.log(whole) - jnp.log(mu_total))
     gq = col_potential_new / EPS + log_col - log_nu_total
     fq = row_potential / EPS

time: 853 us -> 792 us (0.928)
  blocking collectives: 512 us -> 372 us
  waiting for transfers between devices: 51.2 us -> 123 us
    psum x1 -> x0, blocking collectives: 140 us -> none  [on_device(): whole = lax.psum(scaled, 'row')]
    all_gather x0 -> x1, waiting for transfers between devices: none -> 70.8 us  [step_on_ratios(): return jnp.sum(lax.all_gather(block_here, axis_name=peer_axis), axis=0)]
  transfers between devices with their start and end apart: 2 -> 3, of which waited for: 1 -> 2; matrix products, arithmetic and copies ran while one was open for 1% -> 1% of each run, Pallas kernels for 0% -> 0%
where the time goes in v1:
time: 792 us; the launch traced here: 791 us
  blocking collectives  372 us (47%)
  matrix products  174 us (22%)
  waiting for transfers between devices  123 us (16%)
  loops' own time  47.4 us (6%)
  local copies, waits for them, and re-layouts  30.2 us (4%)
  other arithmetic  29.3 us (4%)
  between operations  15.3 us (2%)
    dot_general x24, matrix products, scores(): lax.dot_general(query, y_float, (((1,), (1,)), ((), ())), precision=lax.P...  163 us
    pmax x1, blocking collectives, on_device(): peak = lax.pmax(col_top, 'row')  136 us
    psum x1, blocking collectives, on_device(): lax.psum((jnp.sum(row_mass.astype(jnp.float32)), jnp.sum(col_mass.astype(...  79.4 us
    all_gather x1, waiting for transfers between devices, step_on_ratios(): return jnp.sum(lax.all_gather(block_here, axis_name=peer_axis), axis=0)  70.8 us
    psum x1, waiting for transfers between devices, on_device(): both_all, mass_all = lax.psum((both, mass), 'col')  52.5 us
    all_gather x1, blocking collectives, on_device(): lax.all_gather(col_mass, 'row', axis=0, tiled=True)  42.5 us
    all_gather x1, blocking collectives, on_device(): lax.all_gather(col_potential, 'row', axis=0, tiled=True)  40.6 us
    all_gather x2, blocking collectives, joined(): pieces = jax.tree.map(lambda part: lax.all_gather(part, axis), value)  26 us
  transfers between devices with their start and end apart: 3, of which 2 were waited for; matrix products, arithmetic and copies ran while one was open for 1% of the time, Pallas kernels for 0%

profile of v1, /device:TPU:2, one launch (start us, length us, event | category | flops | bytes accessed | tf_op | source)
XLA Modules:
  0.0 790.8 jit_solution(12919937706743794005)
XLA Ops:
  7.2 1.5 copy.21
  11.3 79.4 %all-reduce = (f32[]{:T(128)}, f32[]{:T(128)}) all-reduce(f32[]{:T(128)} %convert_reduce_fusion.1, f32[]{:T(128)} %convert_reduce_fusion.2), channel_id=1, replica_groups=mesh['row'=32,'col'=8] {'row','col'}, use_global_device_ids=true, to_apply=%region_12.13 | all-reduce | flops 2 | bytes 16 | tf_op jit(solution)/shard_map/psum | solution.py:106
  94.3 42.5 %all-gather.2 = bf16[32,1,256]{2,1,0:T(2,128)(2,1)S(1)} all-gather(bf16[1,1,256]{2,1,0:T(2,128)(2,1)S(1)} %reshape.39), channel_id=1, replica_groups=mesh['row'=32,'col'=8] {'row'}, dimensions={0}, use_global_device_ids=true | all-gather | bytes 16896 | tf_op jit(solution)/shard_map/all_gather | solution.py:69
  136.8 40.6 %all-gather.1 = bf16[32,1,256]{2,1,0:T(2,128)(2,1)S(1)} all-gather(bf16[1,1,256]{2,1,0:T(2,128)(2,1)S(1)} %reshape.37), channel_id=1, replica_groups=mesh['row'=32,'col'=8] {'row'}, dimensions={0}, use_global_device_ids=true | all-gather | bytes 16896 | tf_op jit(solution)/shard_map/all_gather | solution.py:68
  177.5 9.2 %all-gather.5 = bf16[8,1,128]{2,1,0:T(2,128)(2,1)S(1)} all-gather(bf16[1,1,128]{2,1,0:T(2,128)(2,1)} %bitcast.86), channel_id=1, replica_groups=mesh['row'=32,'col'=8] {'col'}, dimensions={0}, use_global_device_ids=true | all-gather | bytes 2304 | tf_op jit(solution)/shard_map/all_gather | solution.py:64
  186.7 12.8 %all_gather.30 = bf16[1024,64]{1,0:T(8,128)(2,1)S(1)} all-gather(bf16[128,64]{1,0:T(8,128)(2,1)S(1)} %copy.19), channel_id=1, replica_groups=mesh['row'=32,'col'=8] {'col'}, dimensions={0}, use_global_device_ids=true | all-gather | bytes 147456 | tf_op jit(solution)/shard_map/all_gather | solution.py:63
  199.5 12.8 %all_gather.31 = bf16[1024,64]{1,0:T(8,128)(2,1)S(1)} all-gather(bf16[128,64]{1,0:T(8,128)(2,1)S(1)} %copy.20), channel_id=1, replica_groups=mesh['row'=32,'col'=8] {'col'}, dimensions={0}, use_global_device_ids=true | all-gather | bytes 147456 | tf_op jit(solution)/shard_map/all_gather | solution.py:62
  213.6 5.2 multiply_reduce_fusion
  218.8 2.2 convert_element_type.39
  221.0 80.0 %while.48 = (s32[]{:T(128)}, f32[8,128]{1,0:T(8,128)S(1)}, f32[8,128]{1,0:T(8,128)S(1)}, s32[8]{0:T(128)S(1)}, f32[1024,64]{1,0:T(8,128)S(1)}, /*index=5*/f32[81...) while((s32[]{:T(128)}, f32[8,128]{1,0:T(8,128)S(1)}, ...), condition=%wide.region_8.9_spmd, body=%wide.region_5.8_spmd.sunk | while | flops 815791872 | bytes 10656463 | solution.py:103
  223.7 6.5 fusion.52
  233.7 6.5 fusion.52
  243.7 6.5 fusion.52
  253.7 6.5 fusion.52
  263.7 6.5 fusion.52
  273.7 6.5 fusion.52
  283.7 6.5 fusion.52
  293.7 6.5 fusion.52
  301.0 12.9 %all-gather.3 = f32[8,1,1024]{2,1,0:T(1,128)S(1)} all-gather(f32[1,1,1024]{2,1,0:T(1,128)S(1)} %bitcast.83), channel_id=1, replica_groups=mesh['row'=32,'col'=8] {'col'}, dimensions={0}, use_global_device_ids=true | all-gather | bytes 36864 | tf_op jit(solution)/shard_map/all_gather | solution.py:16
  313.9 13.1 %all-gather.4 = f32[8,1,1024]{2,1,0:T(1,128)S(1)} all-gather(f32[1,1,1024]{2,1,0:T(1,128)S(1)} %bitcast.82), channel_id=1, replica_groups=mesh['row'=32,'col'=8] {'col'}, dimensions={0}, use_global_device_ids=true | all-gather | bytes 36864 | tf_op jit(solution)/shard_map/all_gather | solution.py:16
  328.0 80.8 %while.50 = (s32[]{:T(128)}, f32[8,8192]{1,0:T(8,128)S(1)}, f32[8,8192]{1,0:T(8,128)S(1)}, s32[8]{0:T(128)S(1)}, f32[1024,64]{1,0:T(8,128)S(1)}, /*index=5*/f32[...) while((s32[]{:T(128)}, f32[8,8192]{1,0:T(8,128)S(1)}, ...), condition=%wide.region_16.17_spmd, body=%wide.region_13.16_spmd.sunk | while | flops 815775744 | bytes 10851027 | solution.py:121
  330.7 6.4 fusion.54
  340.8 6.4 fusion.54
  350.9 6.4 fusion.54
  361.0 6.4 fusion.54
  371.1 6.4 fusion.54
  381.3 6.4 fusion.54
  391.4 6.4 fusion.54
  401.5 6.4 fusion.54
  408.9 136.0 %pmax.7 = f32[8192]{0:T(1024)S(1)} all-reduce(f32[8192]{0:T(1024)S(1)} %reduce_max.27), channel_id=1, replica_groups=mesh['row'=32,'col'=8] {'row'}, use_global_device_ids=true, to_apply=%region_18.19 | all-reduce | flops 8192 | bytes 65536 | tf_op jit(solution)/shard_map/pmax | solution.py:124
  546.4 3.4 pad_maximum_fusion
  549.8 70.8 %all-gather.11.cloned.1.call-done = f32[262144]{0:T(1024)} async-done(((f32[8192]{0:T(1024)}), f32[262144]{0:T(1024)}) %all-gather.11.cloned.1.call-update) | async-done | bytes 1048592 | tf_op jit(solution)/shard_map/all_gather | solution.py:12
  620.6 1.4 reshape.36
  622.8 93.0 %while.51 = (s32[]{:T(128)}, f32[8,128,128]{2,1,0:T(8,128)}, f32[8,128]{1,0:T(8,128)S(1)}, s32[8]{0:T(128)S(1)}, f32[1024,64]{1,0:T(8,128)}, /*index=5*/f32[8192...) while((s32[]{:T(128)}, f32[8,128,128]{2,1,0:T(8,128)}, ...), condition=%wide.region_25.26_spmd, body=%wide.region_23.25_spmd.sunk | while | flops 1085276032 | bytes 10721507 | solution.py:139
  625.5 7.5 convert_reduce_fusion.4
  637.2 7.5 convert_reduce_fusion.4
  648.8 7.5 convert_reduce_fusion.4
  660.4 7.5 convert_reduce_fusion.4
  672.0 7.5 convert_reduce_fusion.4
  679.5 1.3 fusion.58
  683.6 7.5 convert_reduce_fusion.4
  695.3 7.5 convert_reduce_fusion.4
  706.9 7.5 convert_reduce_fusion.4
  714.4 1.3 fusion.58
  715.8 2.0 copy.23
  717.8 12.4 %psum.31 = f32[1024]{0:T(1024)S(1)} all-reduce(f32[1024]{0:T(1024)S(1)} %bitcast.84), channel_id=1, replica_groups=mesh['row'=32,'col'=8] {'col'}, use_global_device_ids=true, to_apply=%region_27.28 | all-reduce | flops 1024 | bytes 8192 | tf_op jit(solution)/shard_map/psum | solution.py:143
  730.3 52.5 %all-reduce.3.cloned.1.call-done = f32[1024,128]{0,1:T(8,128)} async-done(((f32[1024,128]{0,1:T(8,128)}), f32[1024,128]{0,1:T(8,128)}) %all-reduce.3.cloned.1.call-update) | async-done | bytes 524304 | tf_op jit(solution)/shard_map/psum | solution.py:143
  782.8 1.5 fusion.28
  (215 shorter events, 50.8 us)
Async XLA Ops:
  7.2 206.4 %all-gather.9.cloned.1.call-start = ((), (), s32[]{:S(2)}) async-start(), calls=%async_computation | async-start | bytes 2162688 | tf_op jit(solution)/shard_map/all_gather | solution.py:67
  8.7 611.9 %all-gather.11.cloned.1.call-start = ((), (), s32[]{:S(2)}) async-start(), calls=%async_computation.2 | async-start | bytes 1081344 | tf_op jit(solution)/shard_map/all_gather | solution.py:12
  213.6 5.2 copy-start
  408.8 137.6 %copy-start.1 = (f32[1024,64]{1,0:T(8,128)}, f32[1024,64]{1,0:T(8,128)S(1)}, u32[]{:S(2)}) copy-start(f32[1024,64]{1,0:T(8,128)S(1)} %get-tuple-element.751) | copy-start | bytes 786436
  545.6 237.2 %all-reduce.3.cloned.1.call-start = ((), (), s32[]{:S(2)}) async-start(), calls=%async_computation.1 | async-start | bytes 1048576 | tf_op jit(solution)/shard_map/psum | solution.py:143
  622.8 160.1 %copy-start.2 = (bf16[128,64]{0,1:T(8,128)(2,1)S(1)}, bf16[128,64]{0,1:T(8,128)(2,1)}, u32[]{:S(2)}) copy-start(bf16[128,64]{0,1:T(8,128)(2,1)} %param.16) | copy-start | bytes 49156
  622.8 160.1 %copy-start.3 = (bf16[128,64]{0,1:T(8,128)(2,1)S(1)}, bf16[128,64]{0,1:T(8,128)(2,1)}, u32[]{:S(2)}) copy-start(bf16[128,64]{0,1:T(8,128)(2,1)} %param.20) | copy-start | bytes 49156
  622.8 160.1 %copy-start.4 = (f32[64]{0:T(128)S(1)}, f32[64]{0:T(128)}, u32[]{:S(2)}) copy-start(f32[64]{0:T(128)} %param.23) | copy-start | bytes 772
Sparse Core Ops, SparseCore 0:
  10.6 79.5 all-gather.8
  545.8 74.7 all-gather.10
  717.9 64.8 all-reduce.2
